TPU v7x, 256 devices: a whole 4x4x8 slice. The times are simulated.
256 devices in a mesh: dp: 32 (over x, y, core), mp: 8 (over z).
Axes of the slice: x: 4, y: 4, z: 8, core: 2. Of those that a mesh axis runs over, the one named last changes fastest.
Arguments:
- hidden: bfloat16 [512, 1024], P('dp'), may hold values from -6 to 6
- attn_gain: float32 [1024], replicated, may hold values from 0.25 to 1.75
- w_qkv: bfloat16 [1024, 3, 1024], P(None, None, 'mp'), may hold values from -2 to 2
- w_out: bfloat16 [1024, 1024], P('mp'), may hold values from -0.1875 to 0.1875
- mlp_gain: float32 [1024], replicated, may hold values from 0.25 to 1.75
- w_gate_up: bfloat16 [1024, 2, 4096], P(None, None, 'mp'), may hold values from -0.1875 to 0.1875
- w_down: bfloat16 [4096, 1024], P('mp'), may hold values from -0.09375 to 0.09375
- kv_cache: bfloat16 [2, 4096, 128, 1024], P(None, 'dp', None, 'mp'), may hold values from -9 to 9
- lengths: int32 [512], replicated, may hold values from 1 to 16384, as said below
- page_request: int32 [4096], P('dp'), may hold values from -1 to 511, as said below
- page_index: int32 [4096], P('dp'), may hold values from 0 to 127, as said below
Outputs:
- appended: bfloat16 [2, 512, 1024], P(None, 'dp', 'mp')
- hidden_out: bfloat16 [512, 1024], P('dp')
Inputs may be any that keep to these rules, and one draw needn't show every extreme that they name: `lengths`: 4 requests hold exactly 16384 tokens, the others fewer than 512. `page_request`: each request owns exactly ceil(lengths / 128) pool pages, which may lie on any data devices; -1 marks an empty page. `page_index`: the pages of a request carry the places 0 to ceil(lengths / 128) - 1, each once; empty pages carry 0.
All inputs are finite; a program needn't handle non-finite values.
Results may differ from a plain program's by a relative error of at most 0.0085.
Values may be sent and summed in bfloat16 or wider, within the bound.
No kernel may reach another device: no remote copies, remote signals or barrier semaphores. Data moves between devices by JAX's collectives and lax.ppermute only.
A program may use at most 128 MiB of HBM per device.

v0:
```python
import jax
import jax.numpy as jnp
from jax import lax
from jax.sharding import PartitionSpec as P

HEAD_DIM = 64
PAGE_BLOCK = 8
EPSILON = 1e-05
NEGATIVE = -1e30


def merged_2(value, axis, join):
    pieces = jax.tree.map(lambda part: lax.all_gather(part, axis), value)
    head = jax.tree.map(lambda part: part[0], pieces)
    tail = jax.tree.map(lambda part: part[1:], pieces)
    running, _ = lax.scan(lambda running, piece: (join(running, piece), None), head, tail)
    return running


def rms_norm(values, gain):
    widened = values.astype(jnp.float32)
    mean_square = jnp.mean(widened * widened, axis=-1, keepdims=True)
    return (widened * lax.rsqrt(mean_square + EPSILON) * gain).astype(jnp.bfloat16)


def combine(first, second):
    largest = jnp.maximum(first[0], second[0])
    shrink_first = jnp.exp(first[0] - largest)
    shrink_second = jnp.exp(second[0] - largest)
    totals = first[1] * shrink_first + second[1] * shrink_second
    weighted = first[2] * shrink_first[:, :, None] + second[2] * shrink_second[:, :, None]
    return (largest, totals, weighted)


def body(
    hidden,
    attn_gain,
    w_qkv,
    w_out,
    mlp_gain,
    w_gate_up,
    w_down,
    kv_cache,
    lengths,
    page_request,
    page_index,
):
    local_rows = hidden.shape[0]
    head_cols = w_qkv.shape[2]
    local_heads = head_cols // HEAD_DIM
    pool_pages = kv_cache.shape[1]
    page_len = kv_cache.shape[2]
    data_devices = lax.axis_size("dp")
    requests = local_rows * data_devices
    score_scale = HEAD_DIM ** (-0.5)
    normed = rms_norm(hidden, attn_gain)
    projected = jnp.dot(
        normed, w_qkv.reshape(w_qkv.shape[0], 3 * head_cols), preferred_element_type=jnp.float32
    )
    projected = lax.optimization_barrier(projected.astype(jnp.bfloat16)).reshape(
        local_rows, 3, head_cols
    )
    appended = jnp.stack([projected[:, 1], projected[:, 2]])
    every_query = lax.all_gather(projected[:, 0], "dp", axis=0, tiled=True)
    own_queries = projected[:, 0].reshape(local_rows, local_heads, HEAD_DIM).astype(jnp.float32)
    own_keys = projected[:, 1].reshape(local_rows, local_heads, HEAD_DIM).astype(jnp.float32)
    own_values = projected[:, 2].reshape(local_rows, local_heads, HEAD_DIM).astype(jnp.float32)
    self_scores = jnp.sum(own_queries * own_keys, axis=-1) * score_scale
    home_row = lax.axis_index("dp") * local_rows
    start_max = lax.dynamic_update_slice(
        jnp.full((requests, local_heads), NEGATIVE, jnp.float32), self_scores, (home_row, 0)
    )
    start_totals = lax.dynamic_update_slice(
        jnp.zeros((requests, local_heads), jnp.float32),
        jnp.ones((local_rows, local_heads), jnp.float32),
        (home_row, 0),
    )
    start_weighted = lax.dynamic_update_slice(
        jnp.zeros((requests, local_heads, HEAD_DIM), jnp.float32), own_values, (home_row, 0, 0)
    )
    visit_order = jnp.arange(pool_pages, dtype=jnp.int32)
    trip_count = pool_pages // PAGE_BLOCK
    request_ids = jnp.arange(requests, dtype=jnp.int32)
    offsets = jnp.arange(page_len, dtype=jnp.int32)

    def visit(step_index, carry):
        running_max, totals, weighted = carry
        picked = lax.dynamic_slice_in_dim(visit_order, step_index * PAGE_BLOCK, PAGE_BLOCK, 0)
        fetched = jnp.take(kv_cache, picked, axis=1)
        owners = page_request[picked]
        page_pos = page_index[picked]
        clamped = jnp.maximum(owners, 0)
        chosen_queries = every_query[clamped].reshape(PAGE_BLOCK, local_heads, HEAD_DIM)
        key_rows = fetched[0].reshape(PAGE_BLOCK, page_len, local_heads, HEAD_DIM)
        value_rows = fetched[1].reshape(PAGE_BLOCK, page_len, local_heads, HEAD_DIM)
        scores = (
            jnp.einsum(
                "phd,pthd->pht", chosen_queries, key_rows, preferred_element_type=jnp.float32
            )
            * score_scale
        )
        position = page_pos[:, None] * page_len + offsets[None, :]
        usable = (owners[:, None] >= 0) & (position < lengths[clamped][:, None])
        page_max = jnp.max(jnp.where(usable[:, None, :], scores, NEGATIVE), axis=2)
        raw = jnp.where(usable[:, None, :], jnp.exp(scores - page_max[:, :, None]), 0.0)
        page_total = jnp.sum(raw, axis=2)
        page_sum = jnp.einsum(
            "pht,pthd->phd",
            raw.astype(jnp.bfloat16),
            value_rows,
            preferred_element_type=jnp.float32,
        )
        member = owners[:, None] == request_ids[None, :]
        candidate = jnp.max(jnp.where(member[:, :, None], page_max[:, None, :], NEGATIVE), axis=0)
        new_max = jnp.maximum(running_max, candidate)
        factors = jnp.where(owners[:, None] >= 0, jnp.exp(page_max - new_max[clamped]), 0.0)
        rescale = jnp.exp(running_max - new_max)
        onehot = member.astype(jnp.float32)
        totals = totals * rescale + jnp.einsum(
            "pr,ph->rh", onehot, page_total * factors, precision=lax.Precision.HIGHEST
        )
        weighted = weighted * rescale[:, :, None] + jnp.einsum(
            "pr,phd->rhd", onehot, page_sum * factors[:, :, None], precision=lax.Precision.HIGHEST
        )
        return (new_max, totals, weighted)

    running_max, totals, weighted = lax.fori_loop(
        0, trip_count, visit, (start_max, start_totals, start_weighted)
    )
    merged = merged_2((running_max, totals, weighted), "dp", combine)
    own_totals = lax.dynamic_slice_in_dim(merged[1], home_row, local_rows, 0)
    own_weighted = lax.dynamic_slice_in_dim(merged[2], home_row, local_rows, 0)
    context = (
        (own_weighted / own_totals[:, :, None]).reshape(local_rows, head_cols).astype(jnp.bfloat16)
    )
    attended = lax.psum(jnp.dot(context, w_out, preferred_element_type=jnp.float32), "mp")
    residual = lax.optimization_barrier(
        (hidden.astype(jnp.float32) + attended).astype(jnp.bfloat16)
    )
    normed_mlp = rms_norm(residual, mlp_gain)
    hidden_cols = w_gate_up.shape[2]
    gate_up = jnp.dot(
        normed_mlp,
        w_gate_up.reshape(w_gate_up.shape[0], 2 * hidden_cols),
        preferred_element_type=jnp.float32,
    ).reshape(local_rows, 2, hidden_cols)
    activated = (jax.nn.silu(gate_up[:, 0]) * gate_up[:, 1]).astype(jnp.bfloat16)
    lowered = lax.psum(jnp.dot(activated, w_down, preferred_element_type=jnp.float32), "mp")
    hidden_out = (residual.astype(jnp.float32) + lowered).astype(jnp.bfloat16)
    return (appended, hidden_out)


def solution(mesh):
    return jax.shard_map(
        body,
        mesh=mesh,
        in_specs=(
            P("dp", None),
            P(),
            P(None, None, "mp"),
            P("mp", None),
            P(),
            P(None, None, "mp"),
            P("mp", None),
            P(None, "dp", None, "mp"),
            P(),
            P("dp"),
            P("dp"),
        ),
        out_specs=(P(None, "dp", "mp"), P("dp", None)),
        check_vma=False,
    )
```

profile of v0, /device:TPU:2, one launch (start us, length us, event | category | flops | bytes accessed | tf_op | source)
XLA Modules:
  0.0 589.8 jit_solution(4555764252407409945)
XLA Ops:
  11.2 24.7 %all-gather = bf16[512,1,128]{2,0,1:T(8,128)(2,1)S(1)} all-gather(bf16[16,1,128]{2,0,1:T(8,128)(2,1)S(1)} %copy.113), channel_id=2, replica_groups=mesh['dp'=32,'mp'=8] {'dp'}, dimensions={0}, use_global_device_ids=true | all-gather | bytes 135168 | tf_op jit(solution)/shard_map/all_gather | solution.py:64
  36.7 190.9 %while.35 = (s32[]{:T(128)}, f32[512,2]{0,1:T(2,128)S(1)}, f32[512,2]{0,1:T(2,128)S(1)}, f32[512,2,64]{0,2,1:T(8,128)S(1)}, s32[128]{0:T(128)S(1)}, /*index=5*/s...) while((s32[]{:T(128)}, f32[512,2]{0,1:T(2,128)S(1)}, ...), condition=%wide.region_6.7_spmd.clone.clone, body=%wide.region_2.6_spmd.clone.clone.sunk | while | flops 7361630 | bytes 5361311 | solution.py:127
  41.5 4.0 gather_fusion.2
  53.5 4.0 gather_fusion.2
  65.4 4.0 gather_fusion.2
  77.3 4.0 gather_fusion.2
  89.3 4.0 gather_fusion.2
  101.2 4.0 gather_fusion.2
  113.1 4.0 gather_fusion.2
  125.1 4.0 gather_fusion.2
  137.0 4.0 gather_fusion.2
  148.9 4.0 gather_fusion.2
  160.9 4.0 gather_fusion.2
  172.8 4.0 gather_fusion.2
  184.7 4.0 gather_fusion.2
  220.5 4.0 gather_fusion.2
  228.4 22.8 %all-gather.1 = f32[16384,2]{0,1:T(2,128)S(1)} all-gather(f32[512,2]{0,1:T(2,128)S(1)} %get-tuple-element.259), channel_id=3, replica_groups=mesh['dp'=32,'mp'=8] {'dp'}, dimensions={0}, use_global_device_ids=true | all-gather | bytes 135168 | tf_op jit(solution)/shard_map/all_gather | solution.py:13
  251.2 24.6 %all-gather.2 = f32[16384,2]{0,1:T(2,128)S(1)} all-gather(f32[512,2]{0,1:T(2,128)S(1)} %get-tuple-element.260), channel_id=4, replica_groups=mesh['dp'=32,'mp'=8] {'dp'}, dimensions={0}, use_global_device_ids=true | all-gather | bytes 135168 | tf_op jit(solution)/shard_map/all_gather | solution.py:13
  275.8 12.0 %all-gather.6.cloned.1.call-done = f32[16384,2,64]{0,2,1:T(8,128)} async-done(((f32[512,2,64]{0,2,1:T(8,128)}), f32[16384,2,64]{0,2,1:T(8,128)}) %all-gather.6.cloned.1.call-update) | async-done | bytes 8388624 | tf_op jit(solution)/shard_map/all_gather | solution.py:13
  289.0 7.1 %slice.95 = f32[15872,2,64]{0,2,1:T(8,128)} slice(f32[16384,2,64]{0,2,1:T(8,128)} %all-gather.6.cloned.1.call-done), slice={[512:16384], [0:2], [0:64]} | slice | bytes 16252928 | tf_op jit(solution)/shard_map/slice | solution.py:15
  296.1 19.6 %copy.125 = f32[15872,2,64]{2,1,0:T(2,128)} copy(f32[15872,2,64]{0,2,1:T(8,128)} %slice.95) | data formatting | bytes 16252928 | tf_op jit(solution)/shard_map/while | solution.py:16
  315.7 119.1 %while.34 = (s32[]{:T(128)}, f32[512,2]{0,1:T(2,128)S(1)}, f32[512,2]{0,1:T(2,128)S(1)}, f32[512,2,64]{2,1,0:T(2,128)S(1)}, f32[31,512,2]{1,2,0:T(2,128)S(1)}, /...) while((s32[]{:T(128)}, f32[512,2]{0,1:T(2,128)S(1)}, f32[512,2]{0,1:T(2,128)S(1)}, ...), condition=%wide.region_8.9_spmd, body=%wide.region_7.8_spmd.sunk | while | flops 202754 | bytes 843877 | solution.py:16
  442.4 65.8 %all-reduce.3.cloned.1.call-done = f32[16,1024]{1,0:T(8,128)} async-done(((f32[16,1024]{1,0:T(8,128)}), f32[16,1024]{1,0:T(8,128)}) %all-reduce.3.cloned.1.call-update) | async-done | bytes 65552 | tf_op jit(solution)/shard_map/psum | solution.py:136
  511.4 70.4 %all-reduce.5.cloned.1.call-done = f32[16,1024]{1,0:T(8,128)} async-done(((f32[16,1024]{1,0:T(8,128)}), f32[16,1024]{1,0:T(8,128)}) %all-reduce.5.cloned.1.call-update) | async-done | bytes 65552 | tf_op jit(solution)/shard_map/psum | solution.py:148
  (680 shorter events, 269.6 us)
Async XLA Ops:
  7.2 502.7 %copy-start = (bf16[512,1024]{1,0:T(8,128)(2,1)S(1)}, bf16[512,1024]{1,0:T(8,128)(2,1)}, u32[]{:S(2)}) copy-start(bf16[512,1024]{1,0:T(8,128)(2,1)} %param.21) | copy-start | bytes 3145732
  7.2 280.6 %all-gather.6.cloned.1.call-start = ((), (), s32[]{:S(2)}) async-start(), calls=%async_computation.2 | async-start | bytes 8650752 | tf_op jit(solution)/shard_map/all_gather | solution.py:13
  227.6 0.7 copy-start.1
  228.3 279.9 %all-reduce.3.cloned.1.call-start = ((), (), s32[]{:S(2)}) async-start(), calls=%async_computation | async-start | bytes 131072 | tf_op jit(solution)/shard_map/psum | solution.py:136
  315.6 119.5 %copy-start.3 = (bf16[128,1024]{1,0:T(8,128)(2,1)S(1)}, bf16[128,1024]{1,0:T(8,128)(2,1)}, u32[]{:S(2)}) copy-start(bf16[128,1024]{1,0:T(8,128)(2,1)} %param.18) | copy-start | bytes 786436
  315.7 192.6 %copy-start.2 = (bf16[16,1024]{1,0:T(8,128)(2,1)S(1)}, bf16[16,1024]{1,0:T(8,128)(2,1)}, u32[]{:S(2)}) copy-start(bf16[16,1024]{1,0:T(8,128)(2,1)} %param.15) | copy-start | bytes 98308
  315.7 193.5 %copy-start.4 = (f32[1024]{0:T(1024)S(1)}, f32[1024]{0:T(1024)}, u32[]{:S(2)}) copy-start(f32[1024]{0:T(1024)} %param.19) | copy-start | bytes 12292
  436.0 145.8 %all-reduce.5.cloned.1.call-start = ((), (), s32[]{:S(2)}) async-start(), calls=%async_computation.1 | async-start | bytes 131072 | tf_op jit(solution)/shard_map/psum | solution.py:148
Sparse Core Ops, SparseCore 0:
  228.4 59.3 all-gather.5
  436.1 72.0 all-reduce.2
  510.9 70.8 all-reduce.4
where the time goes:
time: 593 us; the launch traced here: 590 us
  local copies, waits for them, and re-layouts  206 us (35%)
  waiting for transfers between devices  148 us (25%)
  other arithmetic  126 us (21%)
  blocking collectives  72.1 us (12%)
  matrix products  20.3 us (3%)
  between operations  13.9 us (2%)
    add x31, other arithmetic, combine(): first[2] * shrink_first[:, :, None] + second[2] * shrink_second[:, :, None]  108 us
    psum x1, waiting for transfers between devices, body(): lax.psum(jnp.dot(activated, w_down, preferred_element_type=jnp.float32),...  70.4 us
    psum x1, waiting for transfers between devices, body(): lax.psum(jnp.dot(context, w_out, preferred_element_type=jnp.float32), 'mp')  65.8 us
    gather x16, local copies, waits for them, and re-layouts, visit(): fetched = jnp.take(kv_cache, picked, axis=1)  64.4 us
    all_gather x2, blocking collectives, merged_2(): pieces = jax.tree.map(lambda part: lax.all_gather(part, axis), value)  47.4 us
    all_gather x1, blocking collectives, body(): every_query = lax.all_gather(projected[:, 0], 'dp', axis=0, tiled=True)  24.7 us
    gather x16, local copies, waits for them, and re-layouts, visit(): usable = (owners[:, None] >= 0) & (position < lengths[clamped][:, None])  21.2 us
    gather x16, local copies, waits for them, and re-layouts, visit(): owners = page_request[picked]  20.8 us
  transfers between devices with their start and end apart: 3, of which 3 were waited for; matrix products, arithmetic and copies ran while one was open for 1% of the time, Pallas kernels for 0%

commit v1 on v0

--- a/solution.py
+++ b/solution.py
@@ -61,7 +61,9 @@
         local_rows, 3, head_cols
     )
     appended = jnp.stack([projected[:, 1], projected[:, 2]])
-    every_query = lax.all_gather(projected[:, 0], "dp", axis=0, tiled=True)
+    every_query = jnp.concatenate(
+        lax.all_to_all(jnp.stack([projected[:, 0]] * lax.axis_size("dp")), "dp", 0, 0), axis=0
+    )
     own_queries = projected[:, 0].reshape(local_rows, local_heads, HEAD_DIM).astype(jnp.float32)
     own_keys = projected[:, 1].reshape(local_rows, local_heads, HEAD_DIM).astype(jnp.float32)
     own_values = projected[:, 2].reshape(local_rows, local_heads, HEAD_DIM).astype(jnp.float32)

time: 593 us -> 581 us (0.980)
  blocking collectives: 72.1 us -> 46.2 us
  starting transfers between devices: 0.12 us -> 7.75 us
  waiting for transfers between devices: 148 us -> 154 us
    all_gather x1 -> x0, blocking collectives: 24.7 us -> none  [body(): every_query = lax.all_gather(projected[:, 0], 'dp', axis=0, tiled=True)]
    all_to_all x0 -> x1, starting transfers between devices: none -> 7.62 us  [body(): lax.all_to_all(jnp.stack([projected[:, 0]] * lax.axis_size('dp')), 'dp',...]
  transfers between devices with their start and end apart: 3 -> 4, of which waited for: 3 -> 4; matrix products, arithmetic and copies ran while one was open for 1% -> 1% of each run, Pallas kernels for 0% -> 0%
where the time goes in v1:
time: 581 us; the launch traced here: 578 us
  local copies, waits for them, and re-layouts  207 us (36%)
  waiting for transfers between devices  154 us (27%)
  other arithmetic  126 us (22%)
  blocking collectives  46.2 us (8%)
  matrix products  20.4 us (4%)
  between operations  14 us (2%)
  starting transfers between devices  7.75 us (1%)
    add x31, other arithmetic, combine(): first[2] * shrink_first[:, :, None] + second[2] * shrink_second[:, :, None]  108 us
    psum x1, waiting for transfers between devices, body(): lax.psum(jnp.dot(activated, w_down, preferred_element_type=jnp.float32),...  70.4 us
    psum x1, waiting for transfers between devices, body(): lax.psum(jnp.dot(context, w_out, preferred_element_type=jnp.float32), 'mp')  66 us
    gather x16, local copies, waits for them, and re-layouts, visit(): fetched = jnp.take(kv_cache, picked, axis=1)  64.4 us
    all_gather x2, blocking collectives, merged_2(): pieces = jax.tree.map(lambda part: lax.all_gather(part, axis), value)  46.2 us
    gather x16, local copies, waits for them, and re-layouts, visit(): usable = (owners[:, None] >= 0) & (position < lengths[clamped][:, None])  21.2 us
    gather x16, local copies, waits for them, and re-layouts, visit(): owners = page_request[picked]  20.8 us
    gather x16, local copies, waits for them, and re-layouts, visit(): page_pos = page_index[picked]  20.8 us
  transfers between devices with their start and end apart: 4, of which 4 were waited for; matrix products, arithmetic and copies ran while one was open for 1% of the time, Pallas kernels for 0%

profile of v1, /device:TPU:2, one launch (start us, length us, event | category | flops | bytes accessed | tf_op | source)
XLA Modules:
  0.0 577.6 jit_solution(1713984487491552709)
XLA Ops:
  11.4 7.6 %all-to-all-start = ((bf16[32,16,128]{2,1,0:T(8,128)(2,1)}), bf16[32,16,128]{2,1,0:T(8,128)(2,1)S(1)}, u32[]{:S(2)}, u32[]{:S(2)}) async-start(bf16[32,16,128]{2,1,0:T(8,128)(2,1)} %stack.7), calls=%async_computation | async-start | bytes 262144 | tf_op jit(solution)/shard_map/all_to_all | solution.py:65
  20.3 5.3 all-to-all-done
  25.6 190.9 %while.35 = (s32[]{:T(128)}, f32[512,2]{0,1:T(2,128)S(1)}, f32[512,2]{0,1:T(2,128)S(1)}, f32[512,2,64]{0,2,1:T(8,128)S(1)}, s32[128]{0:T(128)S(1)}, /*index=5*/s...) while((s32[]{:T(128)}, f32[512,2]{0,1:T(2,128)S(1)}, ...), condition=%wide.region_6.7_spmd.clone.clone, body=%wide.region_2.6_spmd.clone.clone.sunk | while | flops 7361630 | bytes 5361311 | solution.py:129
  30.5 4.0 gather_fusion.2
  42.4 4.0 gather_fusion.2
  54.3 4.0 gather_fusion.2
  66.3 4.0 gather_fusion.2
  78.2 4.0 gather_fusion.2
  90.1 4.0 gather_fusion.2
  102.1 4.0 gather_fusion.2
  114.0 4.0 gather_fusion.2
  126.0 4.0 gather_fusion.2
  149.8 4.0 gather_fusion.2
  173.7 4.0 gather_fusion.2
  185.6 4.0 gather_fusion.2
  209.5 4.0 gather_fusion.2
  217.3 23.1 %all-gather = f32[16384,2]{0,1:T(2,128)S(1)} all-gather(f32[512,2]{0,1:T(2,128)S(1)} %get-tuple-element.259), channel_id=2, replica_groups=mesh['dp'=32,'mp'=8] {'dp'}, dimensions={0}, use_global_device_ids=true | all-gather | bytes 135168 | tf_op jit(solution)/shard_map/all_gather | solution.py:13
  240.5 23.1 %all-gather.1 = f32[16384,2]{0,1:T(2,128)S(1)} all-gather(f32[512,2]{0,1:T(2,128)S(1)} %get-tuple-element.260), channel_id=3, replica_groups=mesh['dp'=32,'mp'=8] {'dp'}, dimensions={0}, use_global_device_ids=true | all-gather | bytes 135168 | tf_op jit(solution)/shard_map/all_gather | solution.py:13
  263.6 11.8 %all-gather.5.cloned.1.call-done = f32[16384,2,64]{0,2,1:T(8,128)} async-done(((f32[512,2,64]{0,2,1:T(8,128)}), f32[16384,2,64]{0,2,1:T(8,128)}) %all-gather.5.cloned.1.call-update) | async-done | bytes 8388624 | tf_op jit(solution)/shard_map/all_gather | solution.py:13
  276.7 7.1 %slice.95 = f32[15872,2,64]{0,2,1:T(8,128)} slice(f32[16384,2,64]{0,2,1:T(8,128)} %all-gather.5.cloned.1.call-done), slice={[512:16384], [0:2], [0:64]} | slice | bytes 16252928 | tf_op jit(solution)/shard_map/slice | solution.py:15
  283.7 19.6 %copy.122 = f32[15872,2,64]{2,1,0:T(2,128)} copy(f32[15872,2,64]{0,2,1:T(8,128)} %slice.95) | data formatting | bytes 16252928 | tf_op jit(solution)/shard_map/while | solution.py:16
  303.3 119.1 %while.34 = (s32[]{:T(128)}, f32[512,2]{0,1:T(2,128)S(1)}, f32[512,2]{0,1:T(2,128)S(1)}, f32[512,2,64]{2,1,0:T(2,128)S(1)}, f32[31,512,2]{1,2,0:T(2,128)S(1)}, /...) while((s32[]{:T(128)}, f32[512,2]{0,1:T(2,128)S(1)}, f32[512,2]{0,1:T(2,128)S(1)}, ...), condition=%wide.region_8.9_spmd, body=%wide.region_7.8_spmd.sunk | while | flops 202754 | bytes 843877 | solution.py:16
  430.0 66.0 %all-reduce.3.cloned.1.call-done = f32[16,1024]{1,0:T(8,128)} async-done(((f32[16,1024]{1,0:T(8,128)}), f32[16,1024]{1,0:T(8,128)}) %all-reduce.3.cloned.1.call-update) | async-done | bytes 65552 | tf_op jit(solution)/shard_map/psum | solution.py:138
  499.2 70.4 %all-reduce.5.cloned.1.call-done = f32[16,1024]{1,0:T(8,128)} async-done(((f32[16,1024]{1,0:T(8,128)}), f32[16,1024]{1,0:T(8,128)}) %all-reduce.5.cloned.1.call-update) | async-done | bytes 65552 | tf_op jit(solution)/shard_map/psum | solution.py:150
  (682 shorter events, 274.4 us)
Async XLA Ops:
  7.2 490.5 %copy-start = (bf16[512,1024]{1,0:T(8,128)(2,1)S(1)}, bf16[512,1024]{1,0:T(8,128)(2,1)}, u32[]{:S(2)}) copy-start(bf16[512,1024]{1,0:T(8,128)(2,1)} %param.21) | copy-start | bytes 3145732
  11.4 14.2 %all-to-all-start = ((bf16[32,16,128]{2,1,0:T(8,128)(2,1)}), bf16[32,16,128]{2,1,0:T(8,128)(2,1)S(1)}, u32[]{:S(2)}, u32[]{:S(2)}) async-start(bf16[32,16,128]{2,1,0:T(8,128)(2,1)} %stack.7), calls=%async_computation | async-start | bytes 262144 | tf_op jit(solution)/shard_map/all_to_all | solution.py:65
  19.0 256.4 %all-gather.5.cloned.1.call-start = ((), (), s32[]{:S(2)}) async-start(), calls=%async_computation.3 | async-start | bytes 8650752 | tf_op jit(solution)/shard_map/all_gather | solution.py:13
  216.6 0.7 copy-start.1
  217.3 278.7 %all-reduce.3.cloned.1.call-start = ((), (), s32[]{:S(2)}) async-start(), calls=%async_computation.1 | async-start | bytes 131072 | tf_op jit(solution)/shard_map/psum | solution.py:138
  303.3 119.5 %copy-start.3 = (bf16[128,1024]{1,0:T(8,128)(2,1)S(1)}, bf16[128,1024]{1,0:T(8,128)(2,1)}, u32[]{:S(2)}) copy-start(bf16[128,1024]{1,0:T(8,128)(2,1)} %param.18) | copy-start | bytes 786436
  303.3 192.7 %copy-start.2 = (bf16[16,1024]{1,0:T(8,128)(2,1)S(1)}, bf16[16,1024]{1,0:T(8,128)(2,1)}, u32[]{:S(2)}) copy-start(bf16[16,1024]{1,0:T(8,128)(2,1)} %param.15) | copy-start | bytes 98308
  303.3 193.7 %copy-start.4 = (f32[1024]{0:T(1024)S(1)}, f32[1024]{0:T(1024)}, u32[]{:S(2)}) copy-start(f32[1024]{0:T(1024)} %param.19) | copy-start | bytes 12292
  423.6 146.0 %all-reduce.5.cloned.1.call-start = ((), (), s32[]{:S(2)}) async-start(), calls=%async_computation.2 | async-start | bytes 131072 | tf_op jit(solution)/shard_map/psum | solution.py:150
Sparse Core Ops, SparseCore 0:
  217.4 57.9 all-gather.4
  423.7 72.2 all-reduce.2
  498.7 70.8 all-reduce.4
